TPU v7x, 128 devices: a whole 4x4x4 slice. The times are simulated.
128 devices in a mesh: dp: 32 (over x, z, core), fsdp: 4 (over y).
Axes of the slice: x: 4, y: 4, z: 4, core: 2. Of those that a mesh axis runs over, the one named last changes fastest.
Arguments:
- latents: bfloat16 [2816, 8, 8, 320], P(('dp', 'fsdp')), may hold values from -6 to 6
- noise_draw: bfloat16 [2816, 8, 8, 320], P(('dp', 'fsdp')), may hold values from -6 to 6
- timesteps: int32 [2816], P(('dp', 'fsdp')), may hold values from 0 to 999
- buckets: int32 [2816], P(('dp', 'fsdp')), may hold values from 0 to 2
- owners: int32 [2816], P(('dp', 'fsdp')), may hold values from 0 to 31, as said below
- adv_grad: bfloat16 [2816, 8, 8, 320], P(('dp', 'fsdp')), may hold values from -6 to 6
- w_down: bfloat16 [2880, 640], P('fsdp'), may hold values from -0.109375 to 0.109375
- w_up: bfloat16 [5760, 320], P('fsdp'), may hold values from -0.078125 to 0.078125
- t_down: bfloat16 [2880, 640], P('fsdp'), may hold values from -0.109375 to 0.109375
- t_up: bfloat16 [5760, 320], P('fsdp'), may hold values from -0.078125 to 0.078125
Outputs:
- student_out: bfloat16 [2816, 8, 8, 320], P(('dp', 'fsdp'))
- grad_down: float32 [2880, 640], P('fsdp')
- grad_up: float32 [5760, 320], P('fsdp')
Inputs may be any that keep to these rules, and one draw needn't show every extreme that they name: `owners`: within one index of fsdp every owner receives exactly 22 tiles; at most 2 of one device's tiles name the same owner, and on every device some owner is named exactly 2 times.
All inputs are finite; a program needn't handle non-finite values.
Results may differ from a plain program's by a relative error of at most 0.015.
Values may be sent and summed in bfloat16 or wider, within the bound.
No kernel may reach another device: no remote copies, remote signals or barrier semaphores. Data moves between devices by JAX's collectives and lax.ppermute only.
A program may use at most 320 MiB of HBM per device.

v0:
```python
import jax
import jax.numpy as jnp
from jax import lax
from jax.sharding import PartitionSpec as P

GROUPS = 32
TSTEPS = 1000
distill_weight = 2.5
norm_epsilon = 1e-05


def conv_forward(volume, kernel_rows, stride):
    in_chan = volume.shape[3]
    kernel = kernel_rows.reshape(3, 3, in_chan, kernel_rows.shape[1])
    return lax.conv_general_dilated(
        volume,
        kernel,
        (stride, stride),
        ((1, 1), (1, 1)),
        dimension_numbers=("NHWC", "HWIO", "NHWC"),
        preferred_element_type=jnp.float32,
    )


def kernel_grad(volume, cotangent, stride):
    pad_upper = 1 if stride == 1 else 0
    result_grad = lax.conv_general_dilated(
        volume,
        cotangent,
        (1, 1),
        ((1, pad_upper), (1, pad_upper)),
        rhs_dilation=(stride, stride),
        dimension_numbers=("CHWN", "IHWO", "HWNC"),
        preferred_element_type=jnp.float32,
    )
    return result_grad.reshape(9 * volume.shape[3], cotangent.shape[3])


def width_masks(buckets, tile_side):
    half_side = tile_side // 2
    tile_count = buckets.shape[0]
    columns = jnp.arange(tile_side, dtype=jnp.int32)
    full_mask = (
        columns[None, None, :, None] < (tile_side - 2 * buckets)[:, None, None, None]
    ).astype(jnp.float32)
    full_mask = jnp.broadcast_to(full_mask, (tile_count, tile_side, tile_side, 1))
    half_cols = jnp.arange(half_side, dtype=jnp.int32)
    half_mask = (
        half_cols[None, None, :, None] < (half_side - buckets)[:, None, None, None]
    ).astype(jnp.float32)
    half_mask = jnp.broadcast_to(half_mask, (tile_count, half_side, half_side, 1))
    return (full_mask, half_mask)


def group_stats(hidden, half_mask):
    tile_count, height, breadth, channels = hidden.shape
    grouped = hidden.reshape(tile_count, height * breadth, GROUPS, channels // GROUPS)
    live_weight = half_mask.reshape(tile_count, height * breadth, 1, 1)
    population = jnp.sum(live_weight, axis=(1, 3), keepdims=True) * (channels // GROUPS)
    center = jnp.sum(grouped * live_weight, axis=(1, 3), keepdims=True) / population
    spread = (
        jnp.sum(jnp.square(grouped - center) * live_weight, axis=(1, 3), keepdims=True) / population
    )
    inverse = lax.rsqrt(spread + norm_epsilon)
    normed = ((grouped - center) * inverse).reshape(hidden.shape)
    return (normed, inverse, population)


def group_back(d_norm, normed, inverse, population, half_mask):
    tile_count, height, breadth, channels = d_norm.shape
    grouped_d = d_norm.reshape(tile_count, height * breadth, GROUPS, channels // GROUPS)
    grouped_n = normed.reshape(tile_count, height * breadth, GROUPS, channels // GROUPS)
    live_weight = half_mask.reshape(tile_count, height * breadth, 1, 1)
    mean_first = jnp.sum(grouped_d, axis=(1, 3), keepdims=True) / population
    mean_second = jnp.sum(grouped_d * grouped_n, axis=(1, 3), keepdims=True) / population
    result = live_weight * inverse * (grouped_d - mean_first - grouped_n * mean_second)
    return result.reshape(d_norm.shape)


def upsample(activated):
    return jnp.repeat(jnp.repeat(activated, 2, axis=1), 2, axis=2)


def network(noisy, full_mask, half_mask, down_weight, up_weight):
    hidden = conv_forward(noisy, down_weight, 2)
    normed, inverse, population = group_stats(hidden, half_mask)
    activated = (half_mask * jax.nn.silu(normed)).astype(jnp.bfloat16)
    enlarged = upsample(activated)
    output = conv_forward(enlarged, up_weight, 1)
    student = (full_mask * (noisy.astype(jnp.float32) + output)).astype(jnp.bfloat16)
    return (student, (noisy, normed, inverse, population, activated, enlarged))


def flip_kernel(up_weight):
    up_chan = up_weight.shape[0] // 9
    out_chan = up_weight.shape[1]
    return (
        up_weight.reshape(3, 3, up_chan, out_chan)[::-1, ::-1]
        .transpose(0, 1, 3, 2)
        .reshape(9 * out_chan, up_chan)
    )


def cotangents(student, target, adversarial, full_mask, half_mask, flipped, cached, loss_scale):
    source_in, normed, inverse, population, activated, enlarged = cached
    tile_count, tile_side = (student.shape[0], student.shape[1])
    half_side = tile_side // 2
    d_out = (
        full_mask
        * (
            distill_weight * (student.astype(jnp.float32) - target.astype(jnp.float32))
            + adversarial.astype(jnp.float32)
        )
        * loss_scale
    ).astype(jnp.bfloat16)
    d_up = conv_forward(d_out, flipped, 1)
    d_up = d_up.reshape(tile_count, half_side, 2, half_side, 2, flipped.shape[1])
    d_act = jnp.sum(d_up, axis=(2, 4))
    sigmoid_n = jax.nn.sigmoid(normed)
    d_norm = half_mask * d_act * sigmoid_n * (1.0 + normed * (1.0 - sigmoid_n))
    d_hidden = group_back(d_norm, normed, inverse, population, half_mask).astype(jnp.bfloat16)
    return (d_out, d_hidden)


def on_device(
    latents, noise_draw, timesteps, buckets, owners, adv_grad, w_down, w_up, t_down, t_up
):
    tile_count, tile_side = (latents.shape[0], latents.shape[1])
    dp_count = lax.axis_size("dp")
    fsdp_count = lax.axis_size("fsdp")
    full_mask, half_mask = width_masks(buckets, tile_side)
    alpha_bar = jnp.square(jnp.cos(0.5 * jnp.pi * (timesteps.astype(jnp.float32) + 0.5) / TSTEPS))
    noisy = (
        full_mask
        * (
            jnp.sqrt(alpha_bar)[:, None, None, None] * latents.astype(jnp.float32)
            + jnp.sqrt(1.0 - alpha_bar)[:, None, None, None] * noise_draw.astype(jnp.float32)
        )
    ).astype(jnp.bfloat16)
    peer_cap = max(2, (tile_count + dp_count - 1) // dp_count)
    slot_count = dp_count * peer_cap
    hit_table = (owners[:, None] == jnp.arange(dp_count, dtype=jnp.int32)[None, :]).astype(
        jnp.int32
    )
    before = jnp.cumsum(hit_table, axis=0) - hit_table
    slot_of = owners * peer_cap + jnp.sum(before * hit_table, axis=1)
    slot_hits = slot_of[None, :] == jnp.arange(slot_count, dtype=jnp.int32)[:, None]
    spread_matrix = slot_hits.astype(jnp.bfloat16)
    send_noisy = (
        jnp.dot(spread_matrix, noisy.reshape(tile_count, -1), preferred_element_type=jnp.float32)
        .astype(jnp.bfloat16)
        .reshape(dp_count, peer_cap, -1)
    )
    send_code = jnp.sum(jnp.where(slot_hits, buckets[None, :] + 1, 0), axis=1).reshape(
        dp_count, peer_cap
    )
    teacher_down, teacher_up = (
        lax.all_gather(t_down, "fsdp", axis=0, tiled=True),
        lax.all_gather(t_up, "fsdp", axis=0, tiled=True),
    )
    recv_noisy, recv_code = (
        lax.all_to_all(send_noisy, "dp", split_axis=0, concat_axis=0, tiled=True),
        lax.all_to_all(send_code, "dp", split_axis=0, concat_axis=0, tiled=True),
    )
    flat_code = recv_code.reshape(slot_count)
    live_slot = (flat_code > 0).astype(jnp.int32)
    position = jnp.cumsum(live_slot) - live_slot
    pick_hits = (live_slot[None, :] == 1) & (
        position[None, :] == jnp.arange(tile_count, dtype=jnp.int32)[:, None]
    )
    pick_matrix = pick_hits.astype(jnp.bfloat16)
    own_noisy = (
        jnp.dot(pick_matrix, recv_noisy.reshape(slot_count, -1), preferred_element_type=jnp.float32)
        .astype(jnp.bfloat16)
        .reshape(latents.shape)
    )
    own_buckets = jnp.sum(jnp.where(pick_hits, flat_code[None, :] - 1, 0), axis=1).astype(jnp.int32)
    own_full, own_half = width_masks(own_buckets, tile_side)
    student_down, student_up = (
        lax.all_gather(w_down, "fsdp", axis=0, tiled=True),
        lax.all_gather(w_up, "fsdp", axis=0, tiled=True),
    )
    student, cached = network(own_noisy, own_full, own_half, student_down, student_up)
    target, _ = network(own_noisy, own_full, own_half, teacher_down, teacher_up)
    loss_scale = jnp.float32(1.0 / (tile_count * dp_count * fsdp_count))
    flipped = flip_kernel(student_up)
    d_out, d_hidden = cotangents(
        student, target, adv_grad, own_full, own_half, flipped, cached, loss_scale
    )
    local_down = kernel_grad(cached[0], d_hidden, 2)
    local_up = kernel_grad(cached[5], d_out, 1)
    shard_down, shard_up = (
        lax.psum_scatter(
            local_down.astype(jnp.bfloat16), "fsdp", scatter_dimension=0, tiled=True
        ).astype(jnp.float32),
        lax.psum_scatter(
            local_up.astype(jnp.bfloat16), "fsdp", scatter_dimension=0, tiled=True
        ).astype(jnp.float32),
    )
    grad_down, grad_up = (
        lax.psum(shard_down.astype(jnp.bfloat16), "dp").astype(jnp.float32),
        lax.psum(shard_up.astype(jnp.bfloat16), "dp").astype(jnp.float32),
    )
    return (student, grad_down, grad_up)


def solution(mesh):
    return jax.shard_map(
        on_device,
        mesh=mesh,
        in_specs=(
            P(("dp", "fsdp"), None, None, None),
            P(("dp", "fsdp"), None, None, None),
            P(("dp", "fsdp")),
            P(("dp", "fsdp")),
            P(("dp", "fsdp")),
            P(("dp", "fsdp"), None, None, None),
            P("fsdp", None),
            P("fsdp", None),
            P("fsdp", None),
            P("fsdp", None),
        ),
        out_specs=(P(("dp", "fsdp"), None, None, None), P("fsdp", None), P("fsdp", None)),
        check_vma=False,
    )
```

profile of v0, /device:TPU:1, one launch (start us, length us, event | category | flops | bytes accessed | tf_op | source)
XLA Modules:
  0.0 477.1 jit_solution(6874258647348290337)
XLA Ops:
  10.6 9.4 %all-to-all-start = ((s32[32,1,2]{2,1,0:T(1,128)}), s32[32,1,2]{2,1,0:T(1,128)S(1)}, u32[]{:S(2)}, u32[]{:S(2)}) async-start(s32[32,1,2]{2,1,0:T(1,128)} %bitcast), calls=%async_computation | async-start | bytes 32768 | tf_op jit(solution)/shard_map/all_to_all | solution.py:163
  25.3 3.0 reshape.387
  28.3 7.4 %all-to-all-start.1 = ((bf16[32,2,20480]{2,1,0:T(2,128)(2,1)}), bf16[32,2,20480]{2,1,0:T(2,128)(2,1)S(1)}, u32[]{:S(2)}, u32[]{:S(2)}) async-start(bf16[32,2,20480]{2,1,0:T(2,128)(2,1)} %reshape.387), calls=%async_computation.1 | async-start | bytes 5242880 | tf_op jit(solution)/shard_map/all_to_all | solution.py:162
  38.9 30.7 %all-to-all-done.1 = bf16[32,2,20480]{2,1,0:T(2,128)(2,1)S(1)} async-done(((bf16[32,2,20480]{2,1,0:T(2,128)(2,1)}), bf16[32,2,20480]{2,1,0:T(2,128)(2,1)S(1)}, u32[]{:S(2)}, u32[]{:S(2)}) %all-to-all-start.1) | async-done | bytes 2621472 | tf_op jit(solution)/shard_map/all_to_all | solution.py:162
  75.6 5.3 %fusion.8 = f32[22,4,4,640]{3,0,2,1:T(8,128)S(1)} fusion(bf16[3,3,320,640]{3,2,1,0:T(8,128)(2,1)} %bitcast.49, bf16[22,8,8,320]{3,2,1,0:T(8,128)(2,1)S(1)} %reshape.389), kind=kOutput, calls=%fused_computation.27 | convolution fusion | flops 1090355200 | bytes 5488640 | tf_op jit(solution)/shard_map/conv_general_dilated | solution.py:15
  80.9 21.8 %all-gather.9.cloned.1.call-done = bf16[2880,640]{1,0:T(8,128)(2,1)} async-done(((bf16[720,640]{1,0:T(8,128)(2,1)}), bf16[2880,640]{1,0:T(8,128)(2,1)}) %all-gather.9.cloned.1.call-update) | async-done | bytes 3686416 | tf_op jit(solution)/shard_map/all_gather | solution.py:158
  102.7 5.0 %multiply_reduce_fusion.2 = (f32[22,640]{1,0:T(8,128)S(1)}, f32[22,640]{1,0:T(8,128)S(1)}, f32[22,4,4,640]{3,0,2,1:T(8,128)S(1)}) fusion(f32[22,4]{0,1:T(4,128)S(1)} %fusion.23, f32[22,4,4,640]{3,0,2,1:T(8,128)S(1)} %fusion.8, bf16[3,3,320,640]{3,2,1,0:T(8,128)(2,1)} %bitcast.50, bf16[22,8,8,320]{3,2,1,0:T(8,128)(2,1)S(1)} %reshape.389), kind=kOutput, calls=%fused_computation.18 | convolution fusion | flops 1091228160 | bytes 6502752 | tf_op jit(solution)/shard_map/conv_general_dilated | solution.py:15
  113.2 37.4 %all-gather.11.cloned.1.call-done = bf16[4,1440,320]{1,2,0:T(8,128)(2,1)} async-done(((bf16[1,1440,320]{1,2,0:T(8,128)(2,1)}), bf16[4,1440,320]{1,2,0:T(8,128)(2,1)}) %all-gather.11.cloned.1.call-update) | async-done | bytes 3686416 | tf_op jit(solution)/shard_map/all_gather | solution.py:181
  150.7 6.5 %copy.64 = bf16[4,1440,320]{2,1,0:T(8,128)(2,1)} copy(bf16[4,1440,320]{1,2,0:T(8,128)(2,1)} %all-gather.11.cloned.1.call-done) | data formatting | bytes 7372800 | tf_op jit(solution)/shard_map/all_gather | solution.py:181
  161.8 11.1 %fusion.1 = bf16[22,8,8,320]{3,0,2,1:T(8,128)(2,1)} fusion(bf16[22,8,8,640]{3,0,2,1:T(8,128)(2,1)S(1)} %bitcast.42, bf16[3,3,640,320]{3,2,1,0:T(8,128)(2,1)S(1)} %bitcast.33, f32[22,8]{0,1:T(8,128)S(1)} %copy-done.19, bf16[22,8,8,320]{3,2,1,0:T(8,128)(2,1)S(1)} %copy-done.8), kind=kOutput, calls=%fused_computation.7 | convolution fusion | flops 4363223040 | bytes 7291584 | tf_op jit(solution)/shard_map/conv_general_dilated | solution.py:15
  172.9 25.6 %all-gather.13.cloned.1.call-done = bf16[4,1440,320]{1,2,0:T(8,128)(2,1)} async-done(((bf16[1,1440,320]{1,2,0:T(8,128)(2,1)}), bf16[4,1440,320]{1,2,0:T(8,128)(2,1)}) %all-gather.13.cloned.1.call-update) | async-done | bytes 3686416 | tf_op jit(solution)/shard_map/all_gather | solution.py:159
  198.5 6.3 %copy.67 = bf16[4,1440,320]{2,1,0:T(8,128)(2,1)} copy(bf16[4,1440,320]{1,2,0:T(8,128)(2,1)} %all-gather.13.cloned.1.call-done) | data formatting | bytes 7372800 | tf_op jit(solution)/shard_map/all_gather | solution.py:159
  207.2 12.3 %multiply_convert_fusion = bf16[22,8,8,320]{3,0,2,1:T(8,128)(2,1)S(1)} fusion(bf16[22,8,8,320]{3,0,2,1:T(8,128)(2,1)} %fusion.1, bf16[22,8,8,640]{3,0,2,1:T(8,128)(2,1)S(1)} %bitcast.44, bf16[3,3,640,320]{3,2,1,0:T(8,128)(2,1)S(1)} %bitcast.37, bf16[22,8,8,320]{3,2,1,0:T(8,128)(2,1)} %param.15, f32[22,8]{0,1:T(8,128)S(1)} %copy-done.19, ...), kind=kOutput, calls=%fused_computation.10 | convolution fusion | flops 4367278080 | bytes 9093824 | tf_op jit(solution)/shard_map/conv_general_dilated | solution.py:15
  219.5 10.7 %fusion.27 = f32[22,8,8,640]{3,0,2,1:T(8,128)} fusion(bf16[22,8,8,320]{3,0,2,1:T(8,128)(2,1)S(1)} %multiply_convert_fusion, bf16[3,3,640,320]{3,2,1,0:T(8,128)(2,1)S(1)} %bitcast.36), kind=kOutput, calls=%fused_computation.72 | convolution fusion | flops 4361420800 | bytes 8192000 | tf_op jit(solution)/shard_map/conv_general_dilated | solution.py:15
  230.3 2.5 reduce_sum.161
  242.9 3.6 mul.215
  246.5 7.6 %mul.216 = f32[22,4,4,640]{3,2,1,0:T(4,128)} reshape(f32[22,16,32,20]{3,2,1,0:T(8,128)} %mul.215) | data formatting | bytes 1802240 | tf_op jit(solution)/shard_map/mul | solution.py:76
  254.1 6.4 %convolution_convert_fusion.2 = bf16[3,3,320,640]{3,2,1,0:T(8,128)(2,1)} fusion(bf16[22,8,8,320]{3,2,1,0:T(8,128)(2,1)S(1)} %copy-done.8, f32[22,4,4,640]{3,2,1,0:T(4,128)} %mul.216, f32[22,4,4,640]{3,0,2,1:T(8,128)S(1)} %fusion.8, f32[22,640]{1,0:T(8,128)S(1)} %copy-done.14, f32[22,640]{1,0:T(8,128)S(1)} %copy-done.15, f32[22,640]{1,0:T(8,128)S(1)} %copy-done.12, ...), kind=kOutput, calls=%fused_computation.4 | convolution fusion | flops 1095802880 | bytes 7516512 | tf_op jit(solution)/shard_map/conv_general_dilated | solution.py:27
  262.4 7.9 %convolution_convert_fusion.3 = bf16[3,3,640,320]{2,3,1,0:T(8,128)(2,1)} fusion(bf16[22,8,8,640]{3,0,2,1:T(8,128)(2,1)S(1)} %bitcast.43, bf16[22,8,8,320]{3,0,2,1:T(8,128)(2,1)S(1)} %copy-done.23), kind=kOutput, calls=%fused_computation.5 | convolution fusion | flops 4363264000 | bytes 6389760 | tf_op jit(solution)/shard_map/conv_general_dilated | solution.py:27
  270.3 7.9 %copy.71 = bf16[3,3,640,320]{3,2,1,0:T(8,128)(2,1)} copy(bf16[3,3,640,320]{2,3,1,0:T(8,128)(2,1)} %convolution_convert_fusion.3) | data formatting | bytes 7372800 | tf_op jit(solution)/shard_map/convert_element_type | solution.py:197
  278.3 25.7 %reduce-scatter.3.cloned.1.call-done = bf16[720,640]{1,0:T(8,128)(2,1)} async-done(((bf16[2880,640]{1,0:T(8,128)(2,1)}), bf16[720,640]{1,0:T(8,128)(2,1)}) %reduce-scatter.3.cloned.1.call-update) | async-done | bytes 921616 | tf_op jit(solution)/shard_map/reduce_scatter | solution.py:193
  303.9 50.8 %reduce-scatter.5.cloned.1.call-done = bf16[1440,320]{1,0:T(8,128)(2,1)} async-done(((bf16[5760,320]{1,0:T(8,128)(2,1)}), bf16[1440,320]{1,0:T(8,128)(2,1)}) %reduce-scatter.5.cloned.1.call-update) | async-done | bytes 921616 | tf_op jit(solution)/shard_map/reduce_scatter | solution.py:196
  355.9 110.0 %all-reduce.3.cloned.1.call-done = (bf16[1440,320]{1,0:T(8,128)(2,1)}, bf16[720,640]{1,0:T(8,128)(2,1)}) async-done(((bf16[1440,320]{1,0:T(8,128)(2,1)}, bf16[720,640]{1,0:T(8,128)(2,1)}), (bf16[1440,320]{1,0:T(8,128)(2,1)}, bf16[720,640]{1,0:T(8,128)(2,1)})) %all-reduce.3.cloned.1.call-update) | async-done | bytes 1843216 | tf_op jit(solution)/shard_map/psum | solution.py:202
  465.9 2.6 copy.73
  (137 shorter events, 44.6 us)
Async XLA Ops:
  7.2 12.8 %copy-start.21 = (s32[22]{0:T(128)S(1)}, s32[22]{0:T(128)}, u32[]{:S(2)}) copy-start(s32[22]{0:T(128)} %param.12) | copy-start | bytes 268
  7.2 12.9 %copy-start.6 = (bf16[22,8,8,320]{3,2,1,0:T(8,128)(2,1)S(1)}, bf16[22,8,8,320]{3,2,1,0:T(8,128)(2,1)}, u32[]{:S(2)}) copy-start(bf16[22,8,8,320]{3,2,1,0:T(8,128)(2,1)} %param.10) | copy-start | bytes 2703364
  7.2 12.9 %copy-start.5 = (bf16[22,8,8,320]{3,2,1,0:T(8,128)(2,1)S(1)}, bf16[22,8,8,320]{3,2,1,0:T(8,128)(2,1)}, u32[]{:S(2)}) copy-start(bf16[22,8,8,320]{3,2,1,0:T(8,128)(2,1)} %param.11) | copy-start | bytes 2703364
  7.2 68.4 %all-gather.7.cloned.1.call-start = ((), (), s32[]{:S(2)}) async-start(), calls=%async_computation.4 | async-start | bytes 4608000 | tf_op jit(solution)/shard_map/all_gather | solution.py:180
  7.9 94.7 %all-gather.9.cloned.1.call-start = ((), (), s32[]{:S(2)}) async-start(), calls=%async_computation.5 | async-start | bytes 4608000 | tf_op jit(solution)/shard_map/all_gather | solution.py:158
  8.7 142.0 %all-gather.11.cloned.1.call-start = ((), (), s32[]{:S(2)}) async-start(), calls=%async_computation.8 | async-start | bytes 4915200 | tf_op jit(solution)/shard_map/all_gather | solution.py:181
  10.6 17.7 %all-to-all-start = ((s32[32,1,2]{2,1,0:T(1,128)}), s32[32,1,2]{2,1,0:T(1,128)S(1)}, u32[]{:S(2)}, u32[]{:S(2)}) async-start(s32[32,1,2]{2,1,0:T(1,128)} %bitcast), calls=%async_computation | async-start | bytes 32768 | tf_op jit(solution)/shard_map/all_to_all | solution.py:163
  28.3 41.3 %all-to-all-start.1 = ((bf16[32,2,20480]{2,1,0:T(2,128)(2,1)}), bf16[32,2,20480]{2,1,0:T(2,128)(2,1)S(1)}, u32[]{:S(2)}, u32[]{:S(2)}) async-start(bf16[32,2,20480]{2,1,0:T(2,128)(2,1)} %reshape.387), calls=%async_computation.1 | async-start | bytes 5242880 | tf_op jit(solution)/shard_map/all_to_all | solution.py:162
  35.7 162.9 %all-gather.13.cloned.1.call-start = ((), (), s32[]{:S(2)}) async-start(), calls=%async_computation.9 | async-start | bytes 4915200 | tf_op jit(solution)/shard_map/all_gather | solution.py:159
  36.3 267.6 %reduce-scatter.3.cloned.1.call-start = ((), (), s32[]{:S(2)}) async-start(), calls=%async_computation.6 | async-start | bytes 4608000 | tf_op jit(solution)/shard_map/reduce_scatter | solution.py:193
  38.3 72.8 %copy-start.16 = (f32[22]{0:T(128)}, f32[22]{0:T(128)S(1)}, u32[]{:S(2)}) copy-start(f32[22]{0:T(128)S(1)} %broadcast_multiply_fusion.1) | copy-start | bytes 268
  75.6 27.1 %copy-start.7 = (bf16[22,8,8,320]{3,2,1,0:T(8,128)(2,1)}, bf16[22,8,8,320]{3,2,1,0:T(8,128)(2,1)S(1)}, u32[]{:S(2)}) copy-start(bf16[22,8,8,320]{3,2,1,0:T(8,128)(2,1)S(1)} %reshape.389) | copy-start | bytes 2703364
  157.2 3.2 copy-start.8
  158.8 3.1 copy-start
  158.8 3.1 copy-start.19
  205.0 14.5 %slice-start = ((s8[4423680]{0:T(1024)(128)(4,1)}), s8[4194304]{0:T(1024)(128)(4,1)S(1)}, s32[]{:S(2)}) async-start(s8[4423680]{0:T(1024)(128)(4,1)} %bitcast.34), calls=%async_computation.11 | async-start | bytes 8388608
  207.2 12.4 %slice-start.1 = ((s8[4423680]{0:T(1024)(128)(4,1)}), s8[229376]{0:T(1024)(128)(4,1)S(1)}, s32[]{:S(2)}) async-start(s8[4423680]{0:T(1024)(128)(4,1)} %bitcast.34), calls=%async_computation.12 | async-start | bytes 458752
  219.5 10.8 %copy-start.22 = (bf16[22,8,8,320]{3,0,2,1:T(8,128)(2,1)}, bf16[22,8,8,320]{3,0,2,1:T(8,128)(2,1)S(1)}, u32[]{:S(2)}) copy-start(bf16[22,8,8,320]{3,0,2,1:T(8,128)(2,1)S(1)} %multiply_convert_fusion) | copy-start | bytes 2703364
  232.8 5.2 %copy-start.17 = (f32[22]{0:T(128)S(1)}, f32[22]{0:T(128)}, u32[]{:S(2)}) copy-start(f32[22]{0:T(128)} %copy-done.16) | copy-start | bytes 268
  246.5 7.7 %copy-start.14 = (f32[22,640]{1,0:T(8,128)S(1)}, f32[22,640]{1,0:T(8,128)}, u32[]{:S(2)}) copy-start(f32[22,640]{1,0:T(8,128)} %mul.237) | copy-start | bytes 168964
  246.5 7.7 %copy-start.15 = (f32[22,640]{1,0:T(8,128)S(1)}, f32[22,640]{1,0:T(8,128)}, u32[]{:S(2)}) copy-start(f32[22,640]{1,0:T(8,128)} %sub.115) | copy-start | bytes 168964
  260.6 94.1 %reduce-scatter.5.cloned.1.call-start = ((), (), s32[]{:S(2)}) async-start(), calls=%async_computation.7 | async-start | bytes 5529600 | tf_op jit(solution)/shard_map/reduce_scatter | solution.py:196
  278.2 76.5 %copy-start.4 = (bf16[22,8,8,320]{3,0,2,1:T(8,128)(2,1)S(1)}, bf16[22,8,8,320]{3,0,2,1:T(8,128)(2,1)}, u32[]{:S(2)}) copy-start(bf16[22,8,8,320]{3,0,2,1:T(8,128)(2,1)} %fusion.1) | copy-start | bytes 2703364
  278.2 187.7 %all-reduce.3.cloned.1.call-start = ((), (), s32[]{:S(2)}) async-start(), calls=%async_computation.10 | async-start | bytes 4055040 | tf_op jit(solution)/shard_map/psum | solution.py:202
  (11 other events, 23.8 us)
Sparse Core Ops, SparseCore 0:
  9.7 47.0 all-gather.6
  58.4 44.2 all-gather.8
  104.4 46.2 all-gather.10
  152.2 46.3 all-gather.12
  260.7 43.1 reduce-scatter.2
  306.2 48.4 reduce-scatter.4
  358.1 107.6 all-reduce.2
where the time goes:
time: 482 us; the launch traced here: 477 us
  waiting for transfers between devices  305 us (63%)
  matrix products  63.2 us (13%)
  local copies, waits for them, and re-layouts  62.9 us (13%)
  starting transfers between devices  17.6 us (4%)
  between operations  15.1 us (3%)
  other arithmetic  13.8 us (3%)
    psum x1, waiting for transfers between devices, on_device(): lax.psum(shard_up.astype(jnp.bfloat16), 'dp').astype(jnp.float32)  110 us
    reduce_scatter x1, waiting for transfers between devices, on_device(): lax.psum_scatter(local_up.astype(jnp.bfloat16), 'fsdp', scatter_dimension...  50.8 us
    conv_general_dilated x5, matrix products, conv_forward(): lax.conv_general_dilated(volume, kernel, (stride, stride), ((1, 1), (1, 1...  44.4 us
    all_gather x1, waiting for transfers between devices, on_device(): lax.all_gather(w_up, 'fsdp', axis=0, tiled=True)  37.4 us
    all_to_all x1, waiting for transfers between devices, on_device(): lax.all_to_all(send_noisy, 'dp', split_axis=0, concat_axis=0, tiled=True)  30.7 us
    reduce_scatter x1, waiting for transfers between devices, on_device(): lax.psum_scatter(local_down.astype(jnp.bfloat16), 'fsdp', scatter_dimensi...  25.7 us
    all_gather x1, waiting for transfers between devices, on_device(): lax.all_gather(t_up, 'fsdp', axis=0, tiled=True)  25.6 us
    all_gather x1, waiting for transfers between devices, on_device(): lax.all_gather(t_down, 'fsdp', axis=0, tiled=True)  21.8 us
  transfers between devices with their start and end apart: 9, of which 7 were waited for; matrix products, arithmetic and copies ran while one was open for 14% of the time, Pallas kernels for 0%

commit v1 on v0

--- a/solution.py
+++ b/solution.py
@@ -7,6 +7,22 @@
 TSTEPS = 1000
 distill_weight = 2.5
 norm_epsilon = 1e-05
+
+
+def collect(x, axis, dim):
+    ways, here, step = (lax.axis_size(axis), lax.axis_index(axis), x.shape[dim])
+    shape = [n * ways if d == dim else n for d, n in enumerate(x.shape)]
+    full = lax.dynamic_update_slice_in_dim(jnp.zeros(shape, x.dtype), x, here * step, axis=dim)
+    going_up = going_down = x
+    for far in range(1, ways // 2 + 1):
+        going_up = lax.ppermute(going_up, axis, [(d, (d + 1) % ways) for d in range(ways)])
+        full = lax.dynamic_update_slice_in_dim(full, going_up, (here - far) % ways * step, axis=dim)
+        if 2 * far < ways:
+            going_down = lax.ppermute(going_down, axis, [(d, (d - 1) % ways) for d in range(ways)])
+            full = lax.dynamic_update_slice_in_dim(
+                full, going_down, (here + far) % ways * step, axis=dim
+            )
+    return full
 
 
 def conv_forward(volume, kernel_rows, stride):
@@ -155,7 +171,7 @@
         dp_count, peer_cap
     )
     teacher_down, teacher_up = (
-        lax.all_gather(t_down, "fsdp", axis=0, tiled=True),
+        collect(t_down, "fsdp", 0),
         lax.all_gather(t_up, "fsdp", axis=0, tiled=True),
     )
     recv_noisy, recv_code = (

time: 482 us -> 464 us (0.963)
  waiting for transfers between devices: 305 us -> 259 us
  local copies, waits for them, and re-layouts: 62.9 us -> 75.6 us
  other arithmetic: 13.8 us -> 23.7 us
    ppermute x0 -> x3, waiting for transfers between devices: none -> 52.5 us  [the longest x2 52.5 us: collect(): lax.ppermute(going_up, axis, [(d, (d + 1) % ways) for d in range(ways)])]
    all_gather x1, waiting for transfers between devices: 37.4 us -> 0.01 us  [on_device(): lax.all_gather(w_up, 'fsdp', axis=0, tiled=True)]
    all_to_all x1, waiting for transfers between devices: 30.7 us -> 0.01 us  [on_device(): lax.all_to_all(send_noisy, 'dp', split_axis=0, concat_axis=0, tiled=True)]
    all_gather x1 -> x0, waiting for transfers between devices: 21.8 us -> none  [on_device(): lax.all_gather(t_down, 'fsdp', axis=0, tiled=True)]
    dynamic_update_slice x0 -> x4, local copies, waits for them, and re-layouts: none -> 7.77 us  [the longest x2 4.47 us: collect(): lax.dynamic_update_slice_in_dim(full, going_up, (here - far) % ways * ste...]
    all_gather x1, waiting for transfers between devices: 25.6 us -> 18.2 us  [on_device(): lax.all_gather(t_up, 'fsdp', axis=0, tiled=True)]
    unnamed x54 -> x58, local copies, waits for them, and re-layouts: 10.4 us -> 10.3 us
  transfers between devices with their start and end apart: 9 -> 11, of which waited for: 7 -> 6; matrix products, arithmetic and copies ran while one was open for 14% -> 20% of each run, Pallas kernels for 0% -> 0%
where the time goes in v1:
time: 464 us; the launch traced here: 457 us
  waiting for transfers between devices  259 us (56%)
  local copies, waits for them, and re-layouts  75.6 us (16%)
  matrix products  63.3 us (14%)
  other arithmetic  23.7 us (5%)
  starting transfers between devices  20.3 us (4%)
  between operations  14.9 us (3%)
    psum x1, waiting for transfers between devices, on_device(): lax.psum(shard_up.astype(jnp.bfloat16), 'dp').astype(jnp.float32)  110 us
    ppermute x2, waiting for transfers between devices, collect(): lax.ppermute(going_up, axis, [(d, (d + 1) % ways) for d in range(ways)])  52.5 us
    reduce_scatter x1, waiting for transfers between devices, on_device(): lax.psum_scatter(local_up.astype(jnp.bfloat16), 'fsdp', scatter_dimension...  50.7 us
    conv_general_dilated x5, matrix products, conv_forward(): lax.conv_general_dilated(volume, kernel, (stride, stride), ((1, 1), (1, 1...  44.6 us
    reduce_scatter x1, waiting for transfers between devices, on_device(): lax.psum_scatter(local_down.astype(jnp.bfloat16), 'fsdp', scatter_dimensi...  25.7 us
    all_gather x1, waiting for transfers between devices, on_device(): lax.all_gather(t_up, 'fsdp', axis=0, tiled=True)  18.2 us
    conv_general_dilated x2, matrix products, kernel_grad(): lax.conv_general_dilated(volume, cotangent, (1, 1), ((1, pad_upper), (1,...  14.3 us
    mul x2, local copies, waits for them, and re-layouts, group_back(): live_weight * inverse * (grouped_d - mean_first - grouped_n * mean_second)  11.2 us
  transfers between devices with their start and end apart: 11, of which 6 were waited for; matrix products, arithmetic and copies ran while one was open for 20% of the time, Pallas kernels for 0%

profile of v1, /device:TPU:1, one launch (start us, length us, event | category | flops | bytes accessed | tf_op | source)
XLA Modules:
  0.0 456.9 jit_solution(13810616990987108178)
XLA Ops:
  11.8 9.5 %all-to-all-start = ((s32[32,1,2]{2,1,0:T(1,128)}), s32[32,1,2]{2,1,0:T(1,128)}, u32[]{:S(2)}, u32[]{:S(2)}) async-start(s32[32,1,2]{2,1,0:T(1,128)} %bitcast), calls=%async_computation | async-start | bytes 32768 | tf_op jit(solution)/shard_map/all_to_all | solution.py:179
  28.5 3.0 reshape.387
  31.5 7.5 %all-to-all-start.1 = ((bf16[32,2,20480]{2,1,0:T(2,128)(2,1)}), bf16[32,2,20480]{2,1,0:T(2,128)(2,1)S(1)}, u32[]{:S(2)}, u32[]{:S(2)}) async-start(bf16[32,2,20480]{2,1,0:T(2,128)(2,1)} %reshape.387), calls=%async_computation.1 | async-start | bytes 5242880 | tf_op jit(solution)/shard_map/all_to_all | solution.py:178
  54.7 21.8 %collective-permute-done = bf16[720,640]{1,0:T(8,128)(2,1)} collective-permute-done((bf16[720,640]{1,0:T(8,128)(2,1)S(1)}, bf16[720,640]{1,0:T(8,128)(2,1)}, u32[]{:S(2)}, u32[]{:S(2)}) %collective-permute-start) | collective-permute-done | bytes 921632 | tf_op jit(solution)/shard_map/ppermute | solution.py:18
  83.2 30.7 %collective-permute-done.2 = bf16[720,640]{1,0:T(8,128)(2,1)} collective-permute-done((bf16[720,640]{1,0:T(8,128)(2,1)}, bf16[720,640]{1,0:T(8,128)(2,1)}, u32[]{:S(2)}, u32[]{:S(2)}) %collective-permute-start.2) | collective-permute-done | bytes 921632 | tf_op jit(solution)/shard_map/ppermute | solution.py:18
  116.2 2.5 reshape.388
  122.2 5.3 %fusion.8 = f32[22,4,4,640]{3,0,2,1:T(8,128)S(1)} fusion(bf16[3,3,320,640]{3,2,1,0:T(8,128)(2,1)} %bitcast.49, bf16[22,8,8,320]{3,2,1,0:T(8,128)(2,1)S(1)} %reshape.389), kind=kOutput, calls=%fused_computation.27 | convolution fusion | flops 1090355200 | bytes 5488640 | tf_op jit(solution)/shard_map/conv_general_dilated | solution.py:31
  127.5 5.0 %multiply_reduce_fusion.2 = (f32[22,640]{1,0:T(8,128)S(1)}, f32[22,640]{1,0:T(8,128)S(1)}, f32[22,4,4,640]{3,0,2,1:T(8,128)S(1)}) fusion(f32[22,4]{0,1:T(4,128)S(1)} %fusion.23, f32[22,4,4,640]{3,0,2,1:T(8,128)S(1)} %fusion.8, bf16[3,3,320,640]{3,2,1,0:T(8,128)(2,1)} %bitcast.7, bf16[22,8,8,320]{3,2,1,0:T(8,128)(2,1)S(1)} %reshape.389), kind=kOutput, calls=%fused_computation.18 | convolution fusion | flops 1091228160 | bytes 6502752 | tf_op jit(solution)/shard_map/conv_general_dilated | solution.py:31
  138.1 6.6 %copy.64 = bf16[4,1440,320]{2,1,0:T(8,128)(2,1)} copy(bf16[4,1440,320]{1,2,0:T(8,128)(2,1)} %all-gather.8.cloned.1.call-done) | data formatting | bytes 7372800 | tf_op jit(solution)/shard_map/all_gather | solution.py:197
  149.3 11.1 %fusion.1 = bf16[22,8,8,320]{3,0,2,1:T(8,128)(2,1)} fusion(bf16[22,8,8,640]{3,0,2,1:T(8,128)(2,1)S(1)} %bitcast.42, bf16[3,3,640,320]{3,2,1,0:T(8,128)(2,1)S(1)} %bitcast.33, f32[22,8]{0,1:T(8,128)S(1)} %copy-done.19, bf16[22,8,8,320]{3,2,1,0:T(8,128)(2,1)S(1)} %copy-done.7), kind=kOutput, calls=%fused_computation.7 | convolution fusion | flops 4363223040 | bytes 7291584 | tf_op jit(solution)/shard_map/conv_general_dilated | solution.py:31
  160.4 18.2 %all-gather.10.cloned.1.call-done = bf16[4,1440,320]{1,2,0:T(8,128)(2,1)} async-done(((bf16[1,1440,320]{1,2,0:T(8,128)(2,1)}), bf16[4,1440,320]{1,2,0:T(8,128)(2,1)}) %all-gather.10.cloned.1.call-update) | async-done | bytes 3686416 | tf_op jit(solution)/shard_map/all_gather | solution.py:175
  178.6 6.3 %copy.67 = bf16[4,1440,320]{2,1,0:T(8,128)(2,1)} copy(bf16[4,1440,320]{1,2,0:T(8,128)(2,1)} %all-gather.10.cloned.1.call-done) | data formatting | bytes 7372800 | tf_op jit(solution)/shard_map/all_gather | solution.py:175
  187.2 12.5 %multiply_convert_fusion = bf16[22,8,8,320]{3,0,2,1:T(8,128)(2,1)S(1)} fusion(bf16[22,8,8,320]{3,0,2,1:T(8,128)(2,1)} %fusion.1, bf16[22,8,8,640]{3,0,2,1:T(8,128)(2,1)S(1)} %bitcast.44, bf16[3,3,640,320]{3,2,1,0:T(8,128)(2,1)S(1)} %bitcast.37, bf16[22,8,8,320]{3,2,1,0:T(8,128)(2,1)} %param.15, f32[22,8]{0,1:T(8,128)S(1)} %copy-done.19, ...), kind=kOutput, calls=%fused_computation.10 | convolution fusion | flops 4367278080 | bytes 9093824 | tf_op jit(solution)/shard_map/conv_general_dilated | solution.py:31
  199.7 10.7 %fusion.27 = f32[22,8,8,640]{3,0,2,1:T(8,128)} fusion(bf16[22,8,8,320]{3,0,2,1:T(8,128)(2,1)S(1)} %multiply_convert_fusion, bf16[3,3,640,320]{3,2,1,0:T(8,128)(2,1)S(1)} %bitcast.36), kind=kOutput, calls=%fused_computation.76 | convolution fusion | flops 4361420800 | bytes 8192000 | tf_op jit(solution)/shard_map/conv_general_dilated | solution.py:31
  210.5 2.5 reduce_sum.161
  223.1 3.6 mul.227
  226.7 7.6 %mul.228 = f32[22,4,4,640]{3,2,1,0:T(4,128)} reshape(f32[22,16,32,20]{3,2,1,0:T(8,128)} %mul.227) | data formatting | bytes 1802240 | tf_op jit(solution)/shard_map/mul | solution.py:92
  234.3 6.4 %convolution_convert_fusion.2 = bf16[3,3,320,640]{3,2,1,0:T(8,128)(2,1)} fusion(bf16[22,8,8,320]{3,2,1,0:T(8,128)(2,1)S(1)} %copy-done.7, f32[22,4,4,640]{3,2,1,0:T(4,128)} %mul.228, f32[22,4,4,640]{3,0,2,1:T(8,128)S(1)} %fusion.8, f32[22,640]{1,0:T(8,128)S(1)} %copy-done.14, f32[22,640]{1,0:T(8,128)S(1)} %copy-done.15, f32[22,640]{1,0:T(8,128)S(1)} %copy-done.12, ...), kind=kOutput, calls=%fused_computation.4 | convolution fusion | flops 1095802880 | bytes 7516512 | tf_op jit(solution)/shard_map/conv_general_dilated | solution.py:43
  242.5 7.9 %convolution_convert_fusion.3 = bf16[3,3,640,320]{2,3,1,0:T(8,128)(2,1)} fusion(bf16[22,8,8,640]{3,0,2,1:T(8,128)(2,1)S(1)} %bitcast.43, bf16[22,8,8,320]{3,0,2,1:T(8,128)(2,1)S(1)} %copy-done.25), kind=kOutput, calls=%fused_computation.5 | convolution fusion | flops 4363264000 | bytes 6389760 | tf_op jit(solution)/shard_map/conv_general_dilated | solution.py:43
  250.4 7.9 %copy.71 = bf16[3,3,640,320]{3,2,1,0:T(8,128)(2,1)} copy(bf16[3,3,640,320]{2,3,1,0:T(8,128)(2,1)} %convolution_convert_fusion.3) | data formatting | bytes 7372800 | tf_op jit(solution)/shard_map/convert_element_type | solution.py:213
  258.4 25.7 %reduce-scatter.3.cloned.1.call-done = bf16[720,640]{1,0:T(8,128)(2,1)} async-done(((bf16[2880,640]{1,0:T(8,128)(2,1)}), bf16[720,640]{1,0:T(8,128)(2,1)}) %reduce-scatter.3.cloned.1.call-update) | async-done | bytes 921616 | tf_op jit(solution)/shard_map/reduce_scatter | solution.py:209
  284.1 50.7 %reduce-scatter.5.cloned.1.call-done = bf16[1440,320]{1,0:T(8,128)(2,1)} async-done(((bf16[5760,320]{1,0:T(8,128)(2,1)}), bf16[1440,320]{1,0:T(8,128)(2,1)}) %reduce-scatter.5.cloned.1.call-update) | async-done | bytes 921616 | tf_op jit(solution)/shard_map/reduce_scatter | solution.py:212
  336.0 109.8 %all-reduce.3.cloned.1.call-done = (bf16[1440,320]{1,0:T(8,128)(2,1)}, bf16[720,640]{1,0:T(8,128)(2,1)}) async-done(((bf16[1440,320]{1,0:T(8,128)(2,1)}, bf16[720,640]{1,0:T(8,128)(2,1)}), (bf16[1440,320]{1,0:T(8,128)(2,1)}, bf16[720,640]{1,0:T(8,128)(2,1)})) %all-reduce.3.cloned.1.call-update) | async-done | bytes 1843216 | tf_op jit(solution)/shard_map/psum | solution.py:218
  445.8 2.6 copy.73
  (149 shorter events, 66.6 us)
Async XLA Ops:
  7.2 14.9 %copy-start.5 = (bf16[22,8,8,320]{3,2,1,0:T(8,128)(2,1)S(1)}, bf16[22,8,8,320]{3,2,1,0:T(8,128)(2,1)}, u32[]{:S(2)}) copy-start(bf16[22,8,8,320]{3,2,1,0:T(8,128)(2,1)} %param.11) | copy-start | bytes 2703364
  7.2 115.0 %all-gather.6.cloned.1.call-start = ((), (), s32[]{:S(2)}) async-start(), calls=%async_computation.4 | async-start | bytes 4608000 | tf_op jit(solution)/shard_map/all_gather | solution.py:196
  7.9 130.2 %all-gather.8.cloned.1.call-start = ((), (), s32[]{:S(2)}) async-start(), calls=%async_computation.7 | async-start | bytes 4915200 | tf_op jit(solution)/shard_map/all_gather | solution.py:197
  11.8 19.7 %all-to-all-start = ((s32[32,1,2]{2,1,0:T(1,128)}), s32[32,1,2]{2,1,0:T(1,128)}, u32[]{:S(2)}, u32[]{:S(2)}) async-start(s32[32,1,2]{2,1,0:T(1,128)} %bitcast), calls=%async_computation | async-start | bytes 32768 | tf_op jit(solution)/shard_map/all_to_all | solution.py:179
  31.5 8.3 %copy-start.10 = (bf16[720,640]{1,0:T(8,128)(2,1)S(1)}, bf16[720,640]{1,0:T(8,128)(2,1)}, u32[]{:S(2)}) copy-start(bf16[720,640]{1,0:T(8,128)(2,1)} %param.18) | copy-start | bytes 2764804
  31.5 84.7 %all-to-all-start.1 = ((bf16[32,2,20480]{2,1,0:T(2,128)(2,1)}), bf16[32,2,20480]{2,1,0:T(2,128)(2,1)S(1)}, u32[]{:S(2)}, u32[]{:S(2)}) async-start(bf16[32,2,20480]{2,1,0:T(2,128)(2,1)} %reshape.387), calls=%async_computation.1 | async-start | bytes 5242880 | tf_op jit(solution)/shard_map/all_to_all | solution.py:178
  39.0 139.6 %all-gather.10.cloned.1.call-start = ((), (), s32[]{:S(2)}) async-start(), calls=%async_computation.8 | async-start | bytes 4915200 | tf_op jit(solution)/shard_map/all_gather | solution.py:175
  39.7 244.3 %reduce-scatter.3.cloned.1.call-start = ((), (), s32[]{:S(2)}) async-start(), calls=%async_computation.5 | async-start | bytes 4608000 | tf_op jit(solution)/shard_map/reduce_scatter | solution.py:209
  39.8 36.7 %collective-permute-start = (bf16[720,640]{1,0:T(8,128)(2,1)S(1)}, bf16[720,640]{1,0:T(8,128)(2,1)}, u32[]{:S(2)}, u32[]{:S(2)}) collective-permute-start(bf16[720,640]{1,0:T(8,128)(2,1)S(1)} %copy-done.10), channel_id=1, source_target_pairs={{0,1},{1,2},{2,3},{3,0},{4,5},{5,6},{6,7},{7,4},{8,9},{9,10},{10,1... | collective-permute-start | bytes 2764808 | tf_op jit(solution)/shard_map/ppermute | solution.py:18
  41.2 39.8 %collective-permute-start.1 = (bf16[720,640]{1,0:T(8,128)(2,1)S(1)}, bf16[720,640]{1,0:T(8,128)(2,1)}, u32[]{:S(2)}, u32[]{:S(2)}) collective-permute-start(bf16[720,640]{1,0:T(8,128)(2,1)S(1)} %copy-done.10), channel_id=1, source_target_pairs={{0,3},{1,0},{2,1},{3,2},{4,7},{5,4},{6,5},{7,6},{8,11},{9,8},{10,9... | collective-permute-start | bytes 2764808 | tf_op jit(solution)/shard_map/ppermute | solution.py:21
  54.0 22.7 %copy-start.20 = (s32[64]{0:T(128)}, s32[64]{0:T(128)S(1)}, u32[]{:S(2)}) copy-start(s32[64]{0:T(128)S(1)} %sub.103) | copy-start | bytes 772
  54.0 22.7 %copy-start.22 = (pred[64]{0:T(512)(128)(4,1)}, pred[64]{0:T(512)(128)(4,1)S(1)}, u32[]{:S(2)}) copy-start(pred[64]{0:T(512)(128)(4,1)S(1)} %broadcast_compare_fusion) | copy-start | bytes 196
  76.5 37.5 %collective-permute-start.2 = (bf16[720,640]{1,0:T(8,128)(2,1)}, bf16[720,640]{1,0:T(8,128)(2,1)}, u32[]{:S(2)}, u32[]{:S(2)}) collective-permute-start(bf16[720,640]{1,0:T(8,128)(2,1)} %collective-permute-done), channel_id=1, source_target_pairs={{0,1},{1,2},{2,3},{3,0},{4,5},{5,6},{6,7},{7,4},{8,9},{9,10},{10,1... | collective-permute-start | bytes 2764808 | tf_op jit(solution)/shard_map/ppermute | solution.py:18
  77.4 56.2 %copy-start.16 = (f32[22]{0:T(128)}, f32[22]{0:T(128)S(1)}, u32[]{:S(2)}) copy-start(f32[22]{0:T(128)S(1)} %broadcast_multiply_fusion.1) | copy-start | bytes 268
  122.1 5.4 %copy-start.6 = (bf16[22,8,8,320]{3,2,1,0:T(8,128)(2,1)}, bf16[22,8,8,320]{3,2,1,0:T(8,128)(2,1)S(1)}, u32[]{:S(2)}) copy-start(bf16[22,8,8,320]{3,2,1,0:T(8,128)(2,1)S(1)} %reshape.389) | copy-start | bytes 2703364
  185.0 14.7 %slice-start = ((s8[4423680]{0:T(1024)(128)(4,1)}), s8[4194304]{0:T(1024)(128)(4,1)S(1)}, s32[]{:S(2)}) async-start(s8[4423680]{0:T(1024)(128)(4,1)} %bitcast.34), calls=%async_computation.10 | async-start | bytes 8388608
  187.2 12.6 %slice-start.1 = ((s8[4423680]{0:T(1024)(128)(4,1)}), s8[229376]{0:T(1024)(128)(4,1)S(1)}, s32[]{:S(2)}) async-start(s8[4423680]{0:T(1024)(128)(4,1)} %bitcast.34), calls=%async_computation.11 | async-start | bytes 458752
  199.7 10.8 %copy-start.24 = (bf16[22,8,8,320]{3,0,2,1:T(8,128)(2,1)}, bf16[22,8,8,320]{3,0,2,1:T(8,128)(2,1)S(1)}, u32[]{:S(2)}) copy-start(bf16[22,8,8,320]{3,0,2,1:T(8,128)(2,1)S(1)} %multiply_convert_fusion) | copy-start | bytes 2703364
  213.0 5.2 %copy-start.18 = (f32[22]{0:T(128)S(1)}, f32[22]{0:T(128)}, u32[]{:S(2)}) copy-start(f32[22]{0:T(128)} %copy-done.16) | copy-start | bytes 268
  226.7 7.6 %copy-start.14 = (f32[22,640]{1,0:T(8,128)S(1)}, f32[22,640]{1,0:T(8,128)}, u32[]{:S(2)}) copy-start(f32[22,640]{1,0:T(8,128)} %mul.253) | copy-start | bytes 168964
  226.7 7.6 %copy-start.15 = (f32[22,640]{1,0:T(8,128)S(1)}, f32[22,640]{1,0:T(8,128)}, u32[]{:S(2)}) copy-start(f32[22,640]{1,0:T(8,128)} %sub.123) | copy-start | bytes 168964
  240.7 94.1 %reduce-scatter.5.cloned.1.call-start = ((), (), s32[]{:S(2)}) async-start(), calls=%async_computation.6 | async-start | bytes 5529600 | tf_op jit(solution)/shard_map/reduce_scatter | solution.py:212
  258.3 76.5 %copy-start.4 = (bf16[22,8,8,320]{3,0,2,1:T(8,128)(2,1)S(1)}, bf16[22,8,8,320]{3,0,2,1:T(8,128)(2,1)}, u32[]{:S(2)}) copy-start(bf16[22,8,8,320]{3,0,2,1:T(8,128)(2,1)} %fusion.1) | copy-start | bytes 2703364
  258.3 187.5 %all-reduce.3.cloned.1.call-start = ((), (), s32[]{:S(2)}) async-start(), calls=%async_computation.9 | async-start | bytes 4055040 | tf_op jit(solution)/shard_map/psum | solution.py:218
  (15 other events, 35.4 us)
Sparse Core Ops, SparseCore 0:
  9.6 59.3 all-gather.5
  70.7 61.5 all-gather.7
  134.0 44.5 all-gather.9
  240.8 43.1 reduce-scatter.2
  286.3 48.4 reduce-scatter.4
  338.1 107.6 all-reduce.2
